TPU v7x, 128 devices: a whole 4x4x4 slice. The times are simulated.
128 devices in a mesh: req: 16 (over x, z), head: 8 (over y, core).
Axes of the slice: x: 4, y: 4, z: 4, core: 2. Of those that a mesh axis runs over, the one named last changes fastest.
Arguments:
- tokens: bfloat16 [16384, 1536], P('req', 'head'), may hold values from -6 to 6
- new_counts: int32 [16, 4], P('req'), may hold values from 1 to 512, 1024 in all within a row
- kv_cache: bfloat16 [64, 8, 7680, 128], P('req', 'head'), may hold values from -300 to 300
- norm_attn: float32 [1536], replicated, may hold values from 0.1 to 1.9
- query_weight: bfloat16 [1536, 8, 192], P(None, 'head'), may hold values from -0.15625 to 0.15625
- key_value_weight: bfloat16 [1536, 8, 128], P(None, 'head'), may hold values from -0.4375 to 0.4375
- output_weight: bfloat16 [8, 192, 1536], P('head'), may hold values from -0.15625 to 0.15625
- norm_moe: float32 [1536], replicated, may hold values from 0.1 to 1.9
- routes: int32 [16384, 8], P(('req', 'head')), may hold values from 0 to 31, all different within a row; in each aligned block of 128 rows (0 to 127, 128 to 255, ...) at most 64 rows name the same one
- route_gain: float32 [16384, 8], P(('req', 'head')), may hold values from 0.03 to 0.3
- w_gate_up: bfloat16 [32, 1536, 1024], P('req'), may hold values from -0.15625 to 0.15625
- w_down: bfloat16 [32, 512, 1536], P('req'), may hold values from -0.25 to 0.25
Outputs:
- mixed: bfloat16 [16384, 1536], P(('req', 'head'))
Inputs may be any that keep to these rules, and one draw needn't show every extreme that they name: `new_counts`: the 4 counts of one index of req sum to 1024, and one of them is exactly 512. `routes`: the 8 experts of a row differ. In each aligned block of 128 rows (the rows of one device) no expert is named more than 64 times, a bound that some block reaches.
All inputs are finite; a program needn't handle non-finite values.
Results may differ from a plain program's by a relative error of at most 0.019.
Values may be sent and summed in bfloat16 or wider, within the bound.
No kernel may reach another device: no remote copies, remote signals or barrier semaphores. Data moves between devices by JAX's collectives and lax.ppermute only.
A program may use at most 128 MiB of HBM per device.

v0:
```python
import math
import jax
import jax.numpy as jnp
from jax import lax
from jax.sharding import PartitionSpec as P

EXPERTS = 32
TOPK = 8
RATIO = 15
floor_score = -1e30


def norm_rows(value_rows, gain_row):
    mean_square = jnp.mean(value_rows * value_rows, axis=-1, keepdims=True)
    return value_rows * lax.rsqrt(mean_square + 1e-05) * gain_row


def rope_tables(position, head_size):
    half_size = head_size // 2
    inverse = jnp.exp(
        jnp.arange(half_size, dtype=jnp.float32) * (-2.0 * math.log(10000.0) / head_size)
    )
    angles = position.astype(jnp.float32)[:, None] * inverse[None, :]
    angles = jnp.concatenate([angles, angles], axis=1)
    return (jnp.cos(angles), jnp.sin(angles))


def rotate(vectors, cos_part, sin_part):
    half_size = vectors.shape[-1] // 2
    turned = jnp.concatenate([-vectors[..., half_size:], vectors[..., :half_size]], axis=-1)
    return vectors * cos_part + turned * sin_part


def request_layout(counts, token_count, cache_ratio):
    end_rows = jnp.cumsum(counts)
    starts = end_rows - counts
    row_ids = jnp.arange(token_count, dtype=jnp.int32)
    segment = jnp.sum((row_ids[:, None] >= end_rows[None, :]).astype(jnp.int32), axis=1)
    member = (segment[:, None] == jnp.arange(counts.shape[0], dtype=jnp.int32)[None, :]).astype(
        jnp.int32
    )
    row_begin = jnp.sum(member * starts[None, :], axis=1)
    own_count = jnp.sum(member * counts[None, :], axis=1)
    position = cache_ratio * own_count + row_ids - row_begin
    return (starts, position)


def project(normed, query_weight, key_value_weight, position):
    token_count, model_width = normed.shape
    kv_heads = key_value_weight.shape[1]
    head_size = key_value_weight.shape[2] // 2
    group_size = query_weight.shape[2] // head_size
    query = jnp.dot(
        normed, query_weight.reshape(model_width, -1), preferred_element_type=jnp.float32
    )
    query = query.reshape(token_count, kv_heads, group_size, head_size)
    keyval = jnp.dot(
        normed, key_value_weight.reshape(model_width, -1), preferred_element_type=jnp.float32
    )
    keyval = keyval.reshape(token_count, kv_heads, 2 * head_size)
    cos_part, sin_part = rope_tables(position, head_size)
    query = rotate(query, cos_part[:, None, None, :], sin_part[:, None, None, :]).astype(
        jnp.bfloat16
    )
    new_key = rotate(keyval[..., :head_size], cos_part[:, None, :], sin_part[:, None, :]).astype(
        jnp.bfloat16
    )
    new_value = keyval[..., head_size:].astype(jnp.bfloat16)
    return (query, new_key, new_value)


def absorb(carried, scores, usable, value_rows, pattern):
    highest, denominator, numerator = carried
    scores = jnp.where(usable, scores, floor_score)
    new_top = jnp.maximum(highest, jnp.max(scores, axis=-1))
    rescale = jnp.exp(highest - new_top)
    weights = jnp.where(usable, jnp.exp(scores - new_top[..., None]), 0.0)
    denominator = denominator * rescale + jnp.sum(weights, axis=-1)
    numerator = numerator * rescale[..., None] + jnp.einsum(
        pattern, weights.astype(jnp.bfloat16), value_rows, preferred_element_type=jnp.float32
    )
    return (new_top, denominator, numerator)


def local(
    tokens,
    new_counts,
    kv_cache,
    norm_attn,
    query_weight,
    key_value_weight,
    output_weight,
    norm_moe,
    routes,
    route_gain,
    w_gate_up,
    w_down,
):
    whole = lax.all_gather(tokens, "head", axis=1, tiled=True)
    token_count, model_width = whole.shape
    normed = norm_rows(whole.astype(jnp.float32), norm_attn).astype(jnp.bfloat16)
    counts = new_counts[0]
    starts, position = request_layout(counts, token_count, RATIO)
    query, new_key, new_value = project(normed, query_weight, key_value_weight, position)
    kv_heads, group_size, head_size = (query.shape[1], query.shape[2], query.shape[3])
    window = token_count // 2
    key_block = 3 * window
    score_scale = 1.0 / math.sqrt(head_size)
    stat_shape = (kv_heads, group_size, window)

    def one_request(which, result):
        row_begin = starts[which]
        count_here = counts[which]
        cached = RATIO * count_here
        win_start = jnp.minimum(row_begin, token_count - window)
        row_ids = win_start + jnp.arange(window, dtype=jnp.int32)
        inside = (row_ids >= row_begin) & (row_ids < row_begin + count_here)
        q_win = lax.dynamic_slice_in_dim(query, win_start, window, 0)
        k_win = lax.dynamic_slice_in_dim(new_key, win_start, window, 0)
        v_win = lax.dynamic_slice_in_dim(new_value, win_start, window, 0)
        p_win = lax.dynamic_slice_in_dim(position, win_start, window, 0)
        past = lax.dynamic_index_in_dim(kv_cache, which, 0, keepdims=False)

        def key_step(block_index, carried):
            key_piece = lax.dynamic_slice_in_dim(past, block_index * key_block, key_block, 1)
            slot_ids = block_index * key_block + jnp.arange(key_block, dtype=jnp.int32)
            usable = (slot_ids < cached)[None, None, None, :]
            scores = (
                jnp.einsum(
                    "qhgd,hkd->hgqk",
                    q_win,
                    key_piece[..., :head_size],
                    preferred_element_type=jnp.float32,
                )
                * score_scale
            )
            return absorb(carried, scores, usable, key_piece[..., head_size:], "hgqk,hkd->hgqd")

        start_state = (
            jnp.full(stat_shape, floor_score, jnp.float32),
            jnp.zeros(stat_shape, jnp.float32),
            jnp.zeros(stat_shape + (head_size,), jnp.float32),
        )
        block_count = (cached + key_block - 1) // key_block
        carried = lax.fori_loop(0, block_count, key_step, start_state)
        new_ok = (inside[None, :] & (p_win[None, :] <= p_win[:, None]))[None, None, :, :]
        scores = (
            jnp.einsum("qhgd,khd->hgqk", q_win, k_win, preferred_element_type=jnp.float32)
            * score_scale
        )
        highest, denominator, numerator = absorb(carried, scores, new_ok, v_win, "hgqk,khd->hgqd")
        attended = jnp.transpose(numerator / denominator[..., None], (2, 0, 1, 3))
        current = lax.dynamic_slice_in_dim(result, win_start, window, 0)
        update = jnp.where(inside[:, None, None, None], attended, current)
        return lax.dynamic_update_slice_in_dim(result, update, win_start, 0)

    initial = jnp.zeros(query.shape, jnp.float32)
    result = lax.fori_loop(0, counts.shape[0], one_request, initial)
    attn_out = result.astype(jnp.bfloat16).reshape(token_count, -1)
    partial_value = jnp.dot(
        attn_out, output_weight.reshape(-1, model_width), preferred_element_type=jnp.float32
    )
    per_block = routes.shape[0]
    row_start = lax.axis_index("head") * per_block
    summed = lax.psum(partial_value.astype(jnp.bfloat16), "head").astype(jnp.float32)
    attn_rows = lax.dynamic_slice_in_dim(summed, row_start, per_block, 0)
    base_rows = lax.dynamic_slice_in_dim(whole, row_start, per_block, 0)
    resid = base_rows.astype(jnp.float32) + attn_rows
    moe_in = norm_rows(resid, norm_moe).astype(jnp.bfloat16)
    capacity = per_block // 2
    flat_routes = routes.reshape(-1)
    expert_ids = jnp.arange(EXPERTS, dtype=jnp.int32)
    onehot = (flat_routes[:, None] == expert_ids[None, :]).astype(jnp.int32)
    before = jnp.cumsum(onehot, axis=0) - onehot
    rank_in = jnp.sum(before * onehot, axis=1)
    slot_ids = flat_routes * capacity + rank_in
    owners = jnp.arange(per_block * TOPK, dtype=jnp.int32) // TOPK
    table = jnp.full((EXPERTS * capacity,), per_block, jnp.int32).at[slot_ids].set(owners)
    padded = jnp.concatenate([moe_in, jnp.zeros((1, model_width), jnp.bfloat16)], axis=0)
    req_count = lax.axis_size("req")
    per_req = w_down.shape[0]
    ff_width = w_down.shape[1]
    outgoing = padded[table].reshape(req_count, per_req, capacity, model_width)
    gate_up = jnp.einsum(
        "sncd,ndf->sncf",
        lax.all_to_all(outgoing, "req", split_axis=0, concat_axis=0, tiled=True),
        w_gate_up,
        preferred_element_type=jnp.float32,
    )
    hidden = (jax.nn.silu(gate_up[..., :ff_width]) * gate_up[..., ff_width:]).astype(jnp.bfloat16)
    produced = jnp.einsum(
        "sncf,nfd->sncd", hidden, w_down, preferred_element_type=jnp.float32
    ).astype(jnp.bfloat16)
    arrived = lax.all_to_all(produced, "req", split_axis=0, concat_axis=0, tiled=True)
    gathered = arrived.reshape(EXPERTS * capacity, model_width)[slot_ids].astype(jnp.float32)
    gathered = gathered.reshape(per_block, TOPK, model_width)
    moe_sum = jnp.sum(gathered * route_gain[..., None], axis=1)
    return (resid + moe_sum).astype(jnp.bfloat16)


def solution(mesh):
    in_specs = (
        P("req", "head"),
        P("req", None),
        P("req", "head", None, None),
        P(),
        P(None, "head", None),
        P(None, "head", None),
        P("head", None, None),
        P(),
        P(("req", "head"), None),
        P(("req", "head"), None),
        P("req", None, None),
        P("req", None, None),
    )
    out_specs = P(("req", "head"), None)
    return jax.shard_map(local, mesh=mesh, in_specs=in_specs, out_specs=out_specs, check_vma=False)
```

profile of v0, /device:TPU:93, one launch (start us, length us, event | category | flops | bytes accessed | tf_op | source)
XLA Modules:
  0.0 638.0 jit_solution(5013867156348235563)
XLA Ops:
  14.4 23.0 %all-gather.2.cloned.1.call-done = bf16[1024,1536]{0,1:T(8,128)(2,1)} async-done(((bf16[1024,192]{0,1:T(8,128)(2,1)}), bf16[1024,1536]{0,1:T(8,128)(2,1)}) %all-gather.2.cloned.1.call-update) | async-done | bytes 3145744 | tf_op jit(solution)/shard_map/all_gather | solution.py:99
  47.8 255.9 %while.88 = (s32[]{:T(128)}, bf16[1024,1,3,64]{0,3,2,1:T(8,128)(2,1)}, s32[4]{0:T(128)S(1)}, s32[4]{0:T(128)S(1)}, bf16[4,1,7680,128]{3,2,1,0:T(8,128)(2,1)}, /*...) while((s32[]{:T(128)}, ...), condition=%wide.region_12.13_spmd, body=%wide.region_5.12_spmd.sunk | while | flops 847329280 | bytes 89355064 | solution.py:158
  59.2 4.0 copy.67
  65.1 12.6 %while.89 = (s32[]{:T(128)}, f32[1,3,512]{2,1,0:T(4,128)S(1)}, f32[1,3,512]{2,1,0:T(4,128)S(1)}, f32[1,3,512,64]{2,3,1,0:T(8,128)}, s32[]{:T(128)}, /*index=5*/s...) while((s32[]{:T(128)}, f32[1,3,512]{2,1,0:T(4,128)S(1)}, ...), condition=%wide.region_9.9_spmd, body=%wide.region_6.8_spmd.sunk | while | flops 634854912 | bytes 67547888 | solution.py:145
  71.6 6.1 fusion.131
  98.3 4.0 copy.67
  104.2 62.9 %while.89 = (s32[]{:T(128)}, f32[1,3,512]{2,1,0:T(4,128)S(1)}, f32[1,3,512]{2,1,0:T(4,128)S(1)}, f32[1,3,512,64]{2,3,1,0:T(8,128)}, s32[]{:T(128)}, /*index=5*/s...) while((s32[]{:T(128)}, f32[1,3,512]{2,1,0:T(4,128)S(1)}, ...), condition=%wide.region_9.9_spmd, body=%wide.region_6.8_spmd.sunk | while | flops 634854912 | bytes 67547888 | solution.py:145
  110.7 6.1 fusion.131
  123.3 6.1 fusion.131
  135.8 6.1 fusion.131
  148.4 6.1 fusion.131
  161.0 6.1 fusion.131
  193.9 25.1 %while.89 = (s32[]{:T(128)}, f32[1,3,512]{2,1,0:T(4,128)S(1)}, f32[1,3,512]{2,1,0:T(4,128)S(1)}, f32[1,3,512,64]{2,3,1,0:T(8,128)}, s32[]{:T(128)}, /*index=5*/s...) while((s32[]{:T(128)}, f32[1,3,512]{2,1,0:T(4,128)S(1)}, ...), condition=%wide.region_9.9_spmd, body=%wide.region_6.8_spmd.sunk | while | flops 634854912 | bytes 67547888 | solution.py:145
  200.4 6.1 fusion.131
  212.9 6.1 fusion.131
  239.0 4.0 copy.67
  244.9 50.3 %while.89 = (s32[]{:T(128)}, f32[1,3,512]{2,1,0:T(4,128)S(1)}, f32[1,3,512]{2,1,0:T(4,128)S(1)}, f32[1,3,512,64]{2,3,1,0:T(8,128)}, s32[]{:T(128)}, /*index=5*/s...) while((s32[]{:T(128)}, f32[1,3,512]{2,1,0:T(4,128)S(1)}, ...), condition=%wide.region_9.9_spmd, body=%wide.region_6.8_spmd.sunk | while | flops 634854912 | bytes 67547888 | solution.py:145
  251.4 6.1 fusion.131
  263.9 6.1 fusion.131
  276.5 6.1 fusion.131
  289.1 6.1 fusion.131
  307.9 9.0 %reduce-window.11 = s32[32,8,128]{2,1,0:T(8,128)S(1)} reduce-window(s32[32,8,128]{2,1,0:T(8,128)S(1)} %fusion.96, s32[]{:T(128)} %constant.233.clone.1), window={size=1x1x128 pad=0_0x0_0x127_0}, to_apply=%region_15.16 | reduce-window | flops 4161536 | bytes 262148 | tf_op jit(solution)/shard_map/reduce-window.1
  317.4 4.3 scatter_custom_fusion
  324.7 52.1 %all-reduce.3.cloned.1.call-done = bf16[1024,1536]{1,0:T(8,128)(2,1)} async-done(((bf16[1024,1536]{1,0:T(8,128)(2,1)}), bf16[1024,1536]{1,0:T(8,128)(2,1)}) %all-reduce.3.cloned.1.call-update) | async-done | bytes 3145744 | tf_op jit(solution)/shard_map/psum | solution.py:165
  380.0 14.3 %gather_fusion = bf16[2048,1536]{1,0:T(8,128)(2,1)} fusion(bf16[129,1536]{1,0:T(8,128)(2,1)} %concatenate.59, s32[2048]{0:T(1024)S(1)} %fusion.98), kind=kCustom, calls=%fused_computation | custom fusion | bytes 12591104 | tf_op jit(solution)/shard_map/gather | solution.py:183
  394.3 76.3 %all_to_all.10 = bf16[16,2,64,1536]{3,2,1,0:T(8,128)(2,1)S(1)} all-to-all(bf16[16,2,64,1536]{3,2,1,0:T(8,128)(2,1)} %bitcast.290), channel_id=1, replica_groups=mesh['req'=16,'head'=8] {'req'}, dimensions={0} | all-to-all | bytes 12582912 | tf_op jit(solution)/shard_map/all_to_all | solution.py:186
  470.6 10.8 %fusion.70 = f32[16,2,64,1024]{3,2,0,1:T(8,128)} fusion(bf16[2,1536,1024]{2,1,0:T(8,128)(2,1)} %param.26, bf16[16,2,64,1536]{3,2,1,0:T(8,128)(2,1)S(1)} %all_to_all.10), kind=kOutput, calls=%fused_computation.81 | convolution fusion | flops 6442450944 | bytes 20971520 | tf_op jit(solution)/shard_map/sncd,ndf->sncf/dot_general | solution.py:184
  481.4 7.3 %convert_bitcast_fusion = bf16[16,2,64,1536]{3,2,0,1:T(8,128)(2,1)S(1)} fusion(bf16[2,512,1536]{2,1,0:T(8,128)(2,1)S(1)} %copy-done, f32[16,2,64,1024]{3,2,0,1:T(8,128)} %fusion.70), kind=kOutput, calls=%fused_computation.77 | convolution fusion | flops 3230662656 | bytes 17825792 | tf_op jit(solution)/shard_map/sncf,nfd->sncd/dot_general | solution.py:191
  491.8 8.0 %all-to-all-start.1 = ((bf16[16,2,64,1536]{3,2,1,0:T(8,128)(2,1)}), bf16[16,2,64,1536]{3,2,1,0:T(8,128)(2,1)}, u32[]{:S(2)}, u32[]{:S(2)}) async-start(bf16[16,2,64,1536]{3,2,1,0:T(8,128)(2,1)} %copy.52), calls=%async_computation.1 | async-start | bytes 12582912 | tf_op jit(solution)/shard_map/all_to_all | solution.py:194
  500.6 113.0 %all-to-all-done.1 = bf16[16,2,64,1536]{3,2,1,0:T(8,128)(2,1)} async-done(((bf16[16,2,64,1536]{3,2,1,0:T(8,128)(2,1)}), bf16[16,2,64,1536]{3,2,1,0:T(8,128)(2,1)}, u32[]{:S(2)}, u32[]{:S(2)}) %all-to-all-start.1) | async-done | bytes 6291488 | tf_op jit(solution)/shard_map/all_to_all | solution.py:194
  613.6 10.9 %gather_fusion.1 = bf16[1024,1536]{1,0:T(8,128)(2,1)} fusion(bf16[2048,1536]{1,0:T(8,128)(2,1)} %bitcast.54, s32[1024]{0:T(1024)S(1)} %broadcast_clamp_fusion), kind=kCustom, calls=%fused_computation.1 | custom fusion | bytes 6295552 | tf_op jit(solution)/shard_map/gather | solution.py:195
  624.5 4.7 fusion.65
  (242 shorter events, 195.1 us)
Async XLA Ops:
  6.5 474.8 %copy-start = (bf16[2,512,1536]{2,1,0:T(8,128)(2,1)S(1)}, bf16[2,512,1536]{2,1,0:T(8,128)(2,1)}, u32[]{:S(2)}) copy-start(bf16[2,512,1536]{2,1,0:T(8,128)(2,1)} %param.27) | copy-start | bytes 9437188
  6.5 33.5 %copy-start.12 = (f32[1536]{0:T(1024)S(1)}, f32[1536]{0:T(1024)}, u32[]{:S(2)}) copy-start(f32[1536]{0:T(1024)} %param.19) | copy-start | bytes 18436
  6.5 30.9 %all-gather.2.cloned.1.call-start = ((), (), s32[]{:S(2)}) async-start(), calls=%async_computation.2 | async-start | bytes 3538944 | tf_op jit(solution)/shard_map/all_gather | solution.py:99
  7.3 369.5 %all-reduce.3.cloned.1.call-start = ((), (), s32[]{:S(2)}) async-start(), calls=%async_computation.3 | async-start | bytes 6291456 | tf_op jit(solution)/shard_map/psum | solution.py:165
  40.0 3.9 copy-start.3
  40.0 3.9 copy-start.11
  43.9 2.1 copy-start.4
  43.9 2.1 copy-start.5
  44.9 2.8 copy-start.10
  51.5 0.7 copy-start.2
  68.0 3.6 copy-start.1
  90.6 0.7 copy-start.2
  107.0 3.6 copy-start.1
  119.6 3.6 copy-start.1
  132.2 3.6 copy-start.1
  144.8 3.6 copy-start.1
  157.4 3.6 copy-start.1
  180.3 0.7 copy-start.2
  196.7 3.6 copy-start.1
  209.3 3.6 copy-start.1
  231.3 0.7 copy-start.2
  247.7 3.6 copy-start.1
  260.3 3.6 copy-start.1
  272.9 3.6 copy-start.1
  285.5 3.6 copy-start.1
  303.7 3.9 copy-start.8
  303.7 4.1 copy-start.7
  303.7 13.6 %copy-start.6 = (s32[1024]{0:T(1024)S(1)}, s32[1024]{0:T(1024)}, u32[]{:S(2)}) copy-start(s32[1024]{0:T(1024)} %eq.41) | copy-start | bytes 12292
  491.8 8.0 %copy-start.9 = (f32[128,8]{0,1:T(8,128)S(1)}, f32[128,8]{0,1:T(8,128)}, u32[]{:S(2)}) copy-start(f32[128,8]{0,1:T(8,128)} %param.25) | copy-start | bytes 12292
  491.8 121.8 %all-to-all-start.1 = ((bf16[16,2,64,1536]{3,2,1,0:T(8,128)(2,1)}), bf16[16,2,64,1536]{3,2,1,0:T(8,128)(2,1)}, u32[]{:S(2)}, u32[]{:S(2)}) async-start(bf16[16,2,64,1536]{3,2,1,0:T(8,128)(2,1)} %copy.52), calls=%async_computation.1 | async-start | bytes 12582912 | tf_op jit(solution)/shard_map/all_to_all | solution.py:194
Sparse Core Ops, SparseCore 0:
  9.0 28.3 all-gather.1
  307.7 69.0 all-reduce.2
where the time goes:
time: 640 us; the launch traced here: 638 us
  waiting for transfers between devices  189 us (30%)
  matrix products  159 us (25%)
  local copies, waits for them, and re-layouts  105 us (16%)
  other arithmetic  76.7 us (12%)
  blocking collectives  76.3 us (12%)
  between operations  13.7 us (2%)
  loops' own time  10.3 us (2%)
  starting transfers between devices  8.06 us (1%)
    all_to_all x1, waiting for transfers between devices, local(): lax.all_to_all(produced, 'req', split_axis=0, concat_axis=0, tiled=True)  113 us
    dot_general x16, matrix products, absorb(): jnp.einsum(pattern, weights.astype(jnp.bfloat16), value_rows, preferred_e...  85.6 us
    all_to_all x1, blocking collectives, local(): lax.all_to_all(outgoing, 'req', split_axis=0, concat_axis=0, tiled=True)  76.3 us
    psum x1, waiting for transfers between devices, local(): lax.psum(partial_value.astype(jnp.bfloat16), 'head').astype(jnp.float32)  52.1 us
    reduce_sum x16, other arithmetic, absorb(): denominator = denominator * rescale + jnp.sum(weights, axis=-1)  45.4 us
    dot_general x12, matrix products, key_step(): jnp.einsum('qhgd,hkd->hgqk', q_win, key_piece[..., :head_size], preferred...  33.6 us
    dynamic_slice x8, local copies, waits for them, and re-layouts, one_request(): past = lax.dynamic_index_in_dim(kv_cache, which, 0, keepdims=False)  27.9 us
    all_gather x1, waiting for transfers between devices, local(): whole = lax.all_gather(tokens, 'head', axis=1, tiled=True)  23 us
  transfers between devices with their start and end apart: 3, of which 3 were waited for; matrix products, arithmetic and copies ran while one was open for 4% of the time, Pallas kernels for 0%

commit v1 on v0

--- a/solution.py
+++ b/solution.py
@@ -191,7 +191,18 @@
     produced = jnp.einsum(
         "sncf,nfd->sncd", hidden, w_down, preferred_element_type=jnp.float32
     ).astype(jnp.bfloat16)
-    arrived = lax.all_to_all(produced, "req", split_axis=0, concat_axis=0, tiled=True)
+    ways, here = (lax.axis_size("req"), lax.axis_index("req"))
+    width = produced.shape[0] // ways
+    shape = list(produced.shape)
+    shape[0] = width
+    height = shape[0]
+    shape[0] = height * ways
+    arrived = jnp.zeros(shape, produced.dtype)
+    for mask in range(ways):
+        part = lax.dynamic_slice_in_dim(produced, (here ^ mask) * width, width, axis=0)
+        if mask:
+            part = lax.ppermute(part, "req", [(d, d ^ mask) for d in range(ways)])
+        arrived = lax.dynamic_update_slice_in_dim(arrived, part, (here ^ mask) * height, axis=0)
     gathered = arrived.reshape(EXPERTS * capacity, model_width)[slot_ids].astype(jnp.float32)
     gathered = gathered.reshape(per_block, TOPK, model_width)
     moe_sum = jnp.sum(gathered * route_gain[..., None], axis=1)

time: 640 us -> 723 us (1.13)
  blocking collectives: 76.3 us -> 0 us
  waiting for transfers between devices: 189 us -> 247 us
  local copies, waits for them, and re-layouts: 105 us -> 159 us
  starting transfers between devices: 8.06 us -> 43.2 us
    all_to_all x1 -> x0, blocking collectives: 76.3 us -> none  [local(): lax.all_to_all(outgoing, 'req', split_axis=0, concat_axis=0, tiled=True)]
    ppermute x0 -> x15, waiting for transfers between devices: none -> 63.9 us  [local(): part = lax.ppermute(part, 'req', [(d, d ^ mask) for d in range(ways)])]
    ppermute x0 -> x15, starting transfers between devices: none -> 36.4 us  [local(): part = lax.ppermute(part, 'req', [(d, d ^ mask) for d in range(ways)])]
    while x44 -> x60, local copies, waits for them, and re-layouts: 11.3 us -> 46 us
    dynamic_update_slice x0 -> x16, local copies, waits for them, and re-layouts: none -> 12.5 us  [local(): lax.dynamic_update_slice_in_dim(arrived, part, (here ^ mask) * height, ax...]
  transfers between devices with their start and end apart: 3 -> 18, of which waited for: 3 -> 13; matrix products, arithmetic and copies ran while one was open for 4% -> 6% of each run, Pallas kernels for 0% -> 0%
where the time goes in v1:
time: 723 us; the launch traced here: 715 us
  waiting for transfers between devices  247 us (34%)
  matrix products  164 us (23%)
  local copies, waits for them, and re-layouts  159 us (22%)
  other arithmetic  77.2 us (11%)
  starting transfers between devices  43.2 us (6%)
  between operations  13.7 us (2%)
  loops' own time  11 us (2%)
    all_to_all x1, waiting for transfers between devices, local(): lax.all_to_all(outgoing, 'req', split_axis=0, concat_axis=0, tiled=True)  108 us
    dot_general x16, matrix products, absorb(): jnp.einsum(pattern, weights.astype(jnp.bfloat16), value_rows, preferred_e...  88.6 us
    ppermute x15, waiting for transfers between devices, local(): part = lax.ppermute(part, 'req', [(d, d ^ mask) for d in range(ways)])  63.9 us
    psum x1, waiting for transfers between devices, local(): lax.psum(partial_value.astype(jnp.bfloat16), 'head').astype(jnp.float32)  52.1 us
    while x60, local copies, waits for them, and re-layouts  46 us
    reduce_sum x16, other arithmetic, absorb(): denominator = denominator * rescale + jnp.sum(weights, axis=-1)  45.2 us
    ppermute x15, starting transfers between devices, local(): part = lax.ppermute(part, 'req', [(d, d ^ mask) for d in range(ways)])  36.4 us
    dot_general x12, matrix products, key_step(): jnp.einsum('qhgd,hkd->hgqk', q_win, key_piece[..., :head_size], preferred...  33.7 us
  transfers between devices with their start and end apart: 18, of which 13 were waited for; matrix products, arithmetic and copies ran while one was open for 6% of the time, Pallas kernels for 0%

profile of v1, /device:TPU:93, one launch (start us, length us, event | category | flops | bytes accessed | tf_op | source)
XLA Modules:
  0.0 714.9 jit_solution(4490140973318029013)
XLA Ops:
  15.0 22.4 %all-gather.2.cloned.1.call-done = bf16[1024,1536]{0,1:T(8,128)(2,1)} async-done(((bf16[1024,192]{0,1:T(8,128)(2,1)}), bf16[1024,1536]{0,1:T(8,128)(2,1)}) %all-gather.2.cloned.1.call-update) | async-done | bytes 3145744 | tf_op jit(solution)/shard_map/all_gather | solution.py:99
  47.6 300.1 %while.88 = (s32[]{:T(128)}, bf16[1024,1,3,64]{0,3,2,1:T(8,128)(2,1)}, s32[4]{0:T(128)}, s32[4]{0:T(128)}, bf16[4,1,7680,128]{3,2,1,0:T(8,128)(2,1)}, /*index=5*...) while((s32[]{:T(128)}, ...), condition=%wide.region_12.13_spmd, body=%wide.region_5.12_spmd.sunk | while | flops 847329280 | bytes 92500848 | solution.py:158
  66.6 15.4 %while.89 = (s32[]{:T(128)}, f32[1,3,512]{2,1,0:T(4,128)S(1)}, f32[1,3,512]{2,1,0:T(4,128)S(1)}, f32[1,3,512,64]{2,3,1,0:T(8,128)}, s32[]{:T(128)}, /*index=5*/s...) while((s32[]{:T(128)}, f32[1,3,512]{2,1,0:T(4,128)S(1)}, ...), condition=%wide.region_9.9_spmd, body=%wide.region_6.8_spmd.sunk | while | flops 634854912 | bytes 67547888 | solution.py:145
  75.9 6.1 fusion.131
  110.9 77.3 %while.89 = (s32[]{:T(128)}, f32[1,3,512]{2,1,0:T(4,128)S(1)}, f32[1,3,512]{2,1,0:T(4,128)S(1)}, f32[1,3,512,64]{2,3,1,0:T(8,128)}, s32[]{:T(128)}, /*index=5*/s...) while((s32[]{:T(128)}, f32[1,3,512]{2,1,0:T(4,128)S(1)}, ...), condition=%wide.region_9.9_spmd, body=%wide.region_6.8_spmd.sunk | while | flops 634854912 | bytes 67547888 | solution.py:145
  120.2 6.1 fusion.131
  135.7 6.1 fusion.131
  151.2 6.1 fusion.131
  166.6 6.1 fusion.131
  182.1 6.1 fusion.131
  217.3 30.9 %while.89 = (s32[]{:T(128)}, f32[1,3,512]{2,1,0:T(4,128)S(1)}, f32[1,3,512]{2,1,0:T(4,128)S(1)}, f32[1,3,512,64]{2,3,1,0:T(8,128)}, s32[]{:T(128)}, /*index=5*/s...) while((s32[]{:T(128)}, f32[1,3,512]{2,1,0:T(4,128)S(1)}, ...), condition=%wide.region_9.9_spmd, body=%wide.region_6.8_spmd.sunk | while | flops 634854912 | bytes 67547888 | solution.py:145
  242.1 6.1 fusion.131
  276.5 61.8 %while.89 = (s32[]{:T(128)}, f32[1,3,512]{2,1,0:T(4,128)S(1)}, f32[1,3,512]{2,1,0:T(4,128)S(1)}, f32[1,3,512,64]{2,3,1,0:T(8,128)}, s32[]{:T(128)}, /*index=5*/s...) while((s32[]{:T(128)}, f32[1,3,512]{2,1,0:T(4,128)S(1)}, ...), condition=%wide.region_9.9_spmd, body=%wide.region_6.8_spmd.sunk | while | flops 634854912 | bytes 67547888 | solution.py:145
  285.8 6.1 fusion.131
  301.3 6.1 fusion.131
  316.7 6.1 fusion.131
  332.2 6.1 fusion.131
  351.8 9.0 %reduce-window.11 = s32[32,8,128]{2,1,0:T(8,128)S(1)} reduce-window(s32[32,8,128]{2,1,0:T(8,128)S(1)} %fusion.96, s32[]{:T(128)} %constant.252.clone.1), window={size=1x1x128 pad=0_0x0_0x127_0}, to_apply=%region_15.16 | reduce-window | flops 4161536 | bytes 262148 | tf_op jit(solution)/shard_map/reduce-window.1
  368.7 52.1 %all-reduce.3.cloned.1.call-done = bf16[1024,1536]{1,0:T(8,128)(2,1)} async-done(((bf16[1024,1536]{1,0:T(8,128)(2,1)}), bf16[1024,1536]{1,0:T(8,128)(2,1)}) %all-reduce.3.cloned.1.call-update) | async-done | bytes 3145744 | tf_op jit(solution)/shard_map/psum | solution.py:165
  424.0 14.3 %gather_fusion = bf16[2048,1536]{1,0:T(8,128)(2,1)} fusion(bf16[129,1536]{1,0:T(8,128)(2,1)} %concatenate.59, s32[2048]{0:T(1024)S(1)} %fusion.98), kind=kCustom, calls=%fused_computation | custom fusion | bytes 12591104 | tf_op jit(solution)/shard_map/gather | solution.py:183
  438.3 6.8 all-to-all-start
  445.8 107.9 %all-to-all-done = bf16[16,2,64,1536]{3,2,1,0:T(8,128)(2,1)} async-done(((bf16[16,2,64,1536]{3,2,1,0:T(8,128)(2,1)}), bf16[16,2,64,1536]{3,2,1,0:T(8,128)(2,1)}, u32[]{:S(2)}, u32[]{:S(2)}) %all-to-all-start) | async-done | bytes 6291488 | tf_op jit(solution)/shard_map/all_to_all | solution.py:186
  553.8 12.6 %fusion.70 = f32[16,2,64,1024]{3,2,0,1:T(8,128)} fusion(bf16[2,1536,1024]{2,1,0:T(8,128)(2,1)} %param.26, bf16[16,2,64,1536]{3,2,1,0:T(8,128)(2,1)} %all-to-all-done), kind=kOutput, calls=%fused_computation.81 | convolution fusion | flops 6442450944 | bytes 20971520 | tf_op jit(solution)/shard_map/sncd,ndf->sncf/dot_general | solution.py:184
  566.3 7.3 %convolution_convert_fusion = bf16[2,16,64,1536]{3,2,1,0:T(8,128)(2,1)S(1)} fusion(bf16[2,512,1536]{2,1,0:T(8,128)(2,1)S(1)} %copy-done, f32[16,2,64,1024]{3,2,0,1:T(8,128)} %fusion.70), kind=kOutput, calls=%fused_computation.77 | convolution fusion | flops 3230662656 | bytes 17825792 | tf_op jit(solution)/shard_map/sncf,nfd->sncd/dot_general | solution.py:191
  585.7 22.6 %collective-permute-done.1 = bf16[1,2,64,1536]{3,2,1,0:T(8,128)(2,1)S(1)} collective-permute-done((bf16[1,2,64,1536]{3,2,1,0:T(8,128)(2,1)S(1)}, bf16[1,2,64,1536]{3,2,1,0:T(8,128)(2,1)S(1)}, u32[]{:S(2)}, u32[]{:S(2)}) %collective-permute-start.1) | collective-permute-done | bytes 393248 | tf_op jit(solution)/shard_map/ppermute | solution.py:204
  624.8 7.2 %collective-permute-start.12 = (bf16[1,2,64,1536]{3,2,1,0:T(8,128)(2,1)S(1)}, bf16[1,2,64,1536]{3,2,1,0:T(8,128)(2,1)S(1)}, u32[]{:S(2)}, u32[]{:S(2)}) collective-permute-start(bf16[1,2,64,1536]{3,2,1,0:T(8,128)(2,1)S(1)} %get-tuple-element.448), channel_id=1, source_target_pairs={{0,104},{8,96},{16,120},{24,112},{32,72},{40,64},{48,88},{56,80},{... | collective-permute-start | bytes 1179656 | tf_op jit(solution)/shard_map/ppermute | solution.py:204
  641.7 8.5 %collective-permute-start.14 = (bf16[1,2,64,1536]{3,2,1,0:T(8,128)(2,1)S(1)}, bf16[1,2,64,1536]{3,2,1,0:T(8,128)(2,1)S(1)}, u32[]{:S(2)}, u32[]{:S(2)}) collective-permute-start(bf16[1,2,64,1536]{3,2,1,0:T(8,128)(2,1)S(1)} %get-tuple-element.446), channel_id=1, source_target_pairs={{0,120},{8,112},{16,104},{24,96},{32,88},{40,80},{48,72},{56,64},{... | collective-permute-start | bytes 1179656 | tf_op jit(solution)/shard_map/ppermute | solution.py:204
  652.1 11.2 %collective-permute-done.11 = bf16[1,2,64,1536]{3,2,1,0:T(8,128)(2,1)S(1)} collective-permute-done((bf16[1,2,64,1536]{3,2,1,0:T(8,128)(2,1)S(1)}, bf16[1,2,64,1536]{3,2,1,0:T(8,128)(2,1)S(1)}, u32[]{:S(2)}, u32[]{:S(2)}) %collective-permute-start.11) | collective-permute-done | bytes 393248 | tf_op jit(solution)/shard_map/ppermute | solution.py:204
  664.1 7.7 %collective-permute-done.12 = bf16[1,2,64,1536]{3,2,1,0:T(8,128)(2,1)S(1)} collective-permute-done((bf16[1,2,64,1536]{3,2,1,0:T(8,128)(2,1)S(1)}, bf16[1,2,64,1536]{3,2,1,0:T(8,128)(2,1)S(1)}, u32[]{:S(2)}, u32[]{:S(2)}) %collective-permute-start.12) | collective-permute-done | bytes 393248 | tf_op jit(solution)/shard_map/ppermute | solution.py:204
  672.5 7.6 %collective-permute-done.13 = bf16[1,2,64,1536]{3,2,1,0:T(8,128)(2,1)S(1)} collective-permute-done((bf16[1,2,64,1536]{3,2,1,0:T(8,128)(2,1)S(1)}, bf16[1,2,64,1536]{3,2,1,0:T(8,128)(2,1)S(1)}, u32[]{:S(2)}, u32[]{:S(2)}) %collective-permute-start.13) | collective-permute-done | bytes 393248 | tf_op jit(solution)/shard_map/ppermute | solution.py:204
  680.9 8.8 %collective-permute-done.14 = bf16[1,2,64,1536]{3,2,1,0:T(8,128)(2,1)S(1)} collective-permute-done((bf16[1,2,64,1536]{3,2,1,0:T(8,128)(2,1)S(1)}, bf16[1,2,64,1536]{3,2,1,0:T(8,128)(2,1)S(1)}, u32[]{:S(2)}, u32[]{:S(2)}) %collective-permute-start.14) | collective-permute-done | bytes 393248 | tf_op jit(solution)/shard_map/ppermute | solution.py:204
  690.6 10.9 %gather_fusion.1 = bf16[1024,1536]{1,0:T(8,128)(2,1)} fusion(bf16[2048,1536]{1,0:T(8,128)(2,1)} %bitcast.69, s32[1024]{0:T(1024)S(1)} %broadcast_clamp_fusion), kind=kCustom, calls=%fused_computation.1 | custom fusion | bytes 6295552 | tf_op jit(solution)/shard_map/gather | solution.py:206
  (302 shorter events, 306.1 us)
Async XLA Ops:
  6.5 559.8 %copy-start = (bf16[2,512,1536]{2,1,0:T(8,128)(2,1)S(1)}, bf16[2,512,1536]{2,1,0:T(8,128)(2,1)}, u32[]{:S(2)}) copy-start(bf16[2,512,1536]{2,1,0:T(8,128)(2,1)} %param.27) | copy-start | bytes 9437188
  6.5 30.9 %all-gather.2.cloned.1.call-start = ((), (), s32[]{:S(2)}) async-start(), calls=%async_computation.1 | async-start | bytes 3538944 | tf_op jit(solution)/shard_map/all_gather | solution.py:99
  7.3 413.5 %all-reduce.3.cloned.1.call-start = ((), (), s32[]{:S(2)}) async-start(), calls=%async_computation.2 | async-start | bytes 6291456 | tf_op jit(solution)/shard_map/psum | solution.py:165
  40.0 3.9 copy-start.5
  40.0 3.9 copy-start.12
  47.6 17.1 %copy-start.3 = (bf16[1024,1,3,64]{0,3,2,1:T(8,128)(2,1)}, bf16[1024,1,3,64]{0,3,2,1:T(8,128)(2,1)S(1)}, u32[]{:S(2)}) copy-start(bf16[1024,1,3,64]{0,3,2,1:T(8,128)(2,1)S(1)} %get-tuple-element.705) | copy-start | bytes 1179652 | tf_op jit(solution)/shard_map/while
  84.7 7.2 %copy-start.4 = (bf16[1024,1,3,64]{0,3,2,1:T(8,128)(2,1)S(1)}, bf16[1024,1,3,64]{0,3,2,1:T(8,128)(2,1)}, u32[]{:S(2)}) copy-start(bf16[1024,1,3,64]{0,3,2,1:T(8,128)(2,1)} %copy-done.3) | copy-start | bytes 1179652 | tf_op jit(solution)/shard_map/while
  91.9 17.1 %copy-start.3 = (bf16[1024,1,3,64]{0,3,2,1:T(8,128)(2,1)}, bf16[1024,1,3,64]{0,3,2,1:T(8,128)(2,1)S(1)}, u32[]{:S(2)}) copy-start(bf16[1024,1,3,64]{0,3,2,1:T(8,128)(2,1)S(1)} %get-tuple-element.705) | copy-start | bytes 1179652 | tf_op jit(solution)/shard_map/while
  190.9 7.5 %copy-start.4 = (bf16[1024,1,3,64]{0,3,2,1:T(8,128)(2,1)S(1)}, bf16[1024,1,3,64]{0,3,2,1:T(8,128)(2,1)}, u32[]{:S(2)}) copy-start(bf16[1024,1,3,64]{0,3,2,1:T(8,128)(2,1)} %copy-done.3) | copy-start | bytes 1179652 | tf_op jit(solution)/shard_map/while
  198.4 17.0 %copy-start.3 = (bf16[1024,1,3,64]{0,3,2,1:T(8,128)(2,1)}, bf16[1024,1,3,64]{0,3,2,1:T(8,128)(2,1)S(1)}, u32[]{:S(2)}) copy-start(bf16[1024,1,3,64]{0,3,2,1:T(8,128)(2,1)S(1)} %get-tuple-element.705) | copy-start | bytes 1179652 | tf_op jit(solution)/shard_map/while
  251.0 6.6 copy-start.4
  257.6 17.0 %copy-start.3 = (bf16[1024,1,3,64]{0,3,2,1:T(8,128)(2,1)}, bf16[1024,1,3,64]{0,3,2,1:T(8,128)(2,1)S(1)}, u32[]{:S(2)}) copy-start(bf16[1024,1,3,64]{0,3,2,1:T(8,128)(2,1)S(1)} %get-tuple-element.705) | copy-start | bytes 1179652 | tf_op jit(solution)/shard_map/while
  341.0 6.6 copy-start.4
  347.7 4.1 copy-start.9
  347.7 13.6 %copy-start.8 = (s32[1024]{0:T(1024)S(1)}, s32[1024]{0:T(1024)}, u32[]{:S(2)}) copy-start(s32[1024]{0:T(1024)} %eq.41) | copy-start | bytes 12292
  438.3 6.8 copy-start.11
  438.3 115.5 %all-to-all-start = ((bf16[16,2,64,1536]{3,2,1,0:T(8,128)(2,1)}), bf16[16,2,64,1536]{3,2,1,0:T(8,128)(2,1)}, u32[]{:S(2)}, u32[]{:S(2)}) async-start(bf16[16,2,64,1536]{3,2,1,0:T(8,128)(2,1)} %bitcast.320), calls=%async_computation | async-start | bytes 12582912 | tf_op jit(solution)/shard_map/all_to_all | solution.py:186
  574.4 10.6 %collective-permute-start = (bf16[1,2,64,1536]{3,2,1,0:T(8,128)(2,1)S(1)}, bf16[1,2,64,1536]{3,2,1,0:T(8,128)(2,1)S(1)}, u32[]{:S(2)}, u32[]{:S(2)}) collective-permute-start(bf16[1,2,64,1536]{3,2,1,0:T(8,128)(2,1)S(1)} %get-tuple-element.460), channel_id=1, source_target_pairs={{0,8},{8,0},{16,24},{24,16},{32,40},{40,32},{48,56},{56,48},{64,72... | collective-permute-start | bytes 1179656 | tf_op jit(solution)/shard_map/ppermute | solution.py:204
  574.5 33.9 %collective-permute-start.1 = (bf16[1,2,64,1536]{3,2,1,0:T(8,128)(2,1)S(1)}, bf16[1,2,64,1536]{3,2,1,0:T(8,128)(2,1)S(1)}, u32[]{:S(2)}, u32[]{:S(2)}) collective-permute-start(bf16[1,2,64,1536]{3,2,1,0:T(8,128)(2,1)S(1)} %get-tuple-element.459), channel_id=1, source_target_pairs={{0,16},{8,24},{16,0},{24,8},{32,48},{40,56},{48,32},{56,40},{64,80... | collective-permute-start | bytes 1179656 | tf_op jit(solution)/shard_map/ppermute | solution.py:204
  574.6 34.6 %collective-permute-start.2 = (bf16[1,2,64,1536]{3,2,1,0:T(8,128)(2,1)S(1)}, bf16[1,2,64,1536]{3,2,1,0:T(8,128)(2,1)S(1)}, u32[]{:S(2)}, u32[]{:S(2)}) collective-permute-start(bf16[1,2,64,1536]{3,2,1,0:T(8,128)(2,1)S(1)} %get-tuple-element.458), channel_id=1, source_target_pairs={{0,24},{8,16},{16,8},{24,0},{32,56},{40,48},{48,40},{56,32},{64,88... | collective-permute-start | bytes 1179656 | tf_op jit(solution)/shard_map/ppermute | solution.py:204
  577.1 32.8 %collective-permute-start.3 = (bf16[1,2,64,1536]{3,2,1,0:T(8,128)(2,1)S(1)}, bf16[1,2,64,1536]{3,2,1,0:T(8,128)(2,1)S(1)}, u32[]{:S(2)}, u32[]{:S(2)}) collective-permute-start(bf16[1,2,64,1536]{3,2,1,0:T(8,128)(2,1)S(1)} %get-tuple-element.457), channel_id=1, source_target_pairs={{0,32},{8,40},{16,48},{24,56},{32,0},{40,8},{48,16},{56,24},{64,96... | collective-permute-start | bytes 1179656 | tf_op jit(solution)/shard_map/ppermute | solution.py:204
  577.1 37.9 %collective-permute-start.4 = (bf16[1,2,64,1536]{3,2,1,0:T(8,128)(2,1)S(1)}, bf16[1,2,64,1536]{3,2,1,0:T(8,128)(2,1)S(1)}, u32[]{:S(2)}, u32[]{:S(2)}) collective-permute-start(bf16[1,2,64,1536]{3,2,1,0:T(8,128)(2,1)S(1)} %get-tuple-element.456), channel_id=1, source_target_pairs={{0,40},{8,32},{16,56},{24,48},{32,8},{40,0},{48,24},{56,16},{64,10... | collective-permute-start | bytes 1179656 | tf_op jit(solution)/shard_map/ppermute | solution.py:204
  584.9 33.3 %collective-permute-start.5 = (bf16[1,2,64,1536]{3,2,1,0:T(8,128)(2,1)S(1)}, bf16[1,2,64,1536]{3,2,1,0:T(8,128)(2,1)S(1)}, u32[]{:S(2)}, u32[]{:S(2)}) collective-permute-start(bf16[1,2,64,1536]{3,2,1,0:T(8,128)(2,1)S(1)} %get-tuple-element.455), channel_id=1, source_target_pairs={{0,48},{8,56},{16,32},{24,40},{32,16},{40,24},{48,0},{56,8},{64,11... | collective-permute-start | bytes 1179656 | tf_op jit(solution)/shard_map/ppermute | solution.py:204
  608.3 11.6 %collective-permute-start.6 = (bf16[1,2,64,1536]{3,2,1,0:T(8,128)(2,1)S(1)}, bf16[1,2,64,1536]{3,2,1,0:T(8,128)(2,1)S(1)}, u32[]{:S(2)}, u32[]{:S(2)}) collective-permute-start(bf16[1,2,64,1536]{3,2,1,0:T(8,128)(2,1)S(1)} %get-tuple-element.454), channel_id=1, source_target_pairs={{0,56},{8,48},{16,40},{24,32},{32,24},{40,16},{48,8},{56,0},{64,12... | collective-permute-start | bytes 1179656 | tf_op jit(solution)/shard_map/ppermute | solution.py:204
  609.1 15.6 %collective-permute-start.7 = (bf16[1,2,64,1536]{3,2,1,0:T(8,128)(2,1)S(1)}, bf16[1,2,64,1536]{3,2,1,0:T(8,128)(2,1)S(1)}, u32[]{:S(2)}, u32[]{:S(2)}) collective-permute-start(bf16[1,2,64,1536]{3,2,1,0:T(8,128)(2,1)S(1)} %get-tuple-element.453), channel_id=1, source_target_pairs={{0,64},{8,72},{16,80},{24,88},{32,96},{40,104},{48,112},{56,120},{... | collective-permute-start | bytes 1179656 | tf_op jit(solution)/shard_map/ppermute | solution.py:204
  609.9 23.3 %collective-permute-start.8 = (bf16[1,2,64,1536]{3,2,1,0:T(8,128)(2,1)S(1)}, bf16[1,2,64,1536]{3,2,1,0:T(8,128)(2,1)S(1)}, u32[]{:S(2)}, u32[]{:S(2)}) collective-permute-start(bf16[1,2,64,1536]{3,2,1,0:T(8,128)(2,1)S(1)} %get-tuple-element.452), channel_id=1, source_target_pairs={{0,72},{8,64},{16,88},{24,80},{32,104},{40,96},{48,120},{56,112},{... | collective-permute-start | bytes 1179656 | tf_op jit(solution)/shard_map/ppermute | solution.py:204
  614.9 26.8 %collective-permute-start.9 = (bf16[1,2,64,1536]{3,2,1,0:T(8,128)(2,1)S(1)}, bf16[1,2,64,1536]{3,2,1,0:T(8,128)(2,1)S(1)}, u32[]{:S(2)}, u32[]{:S(2)}) collective-permute-start(bf16[1,2,64,1536]{3,2,1,0:T(8,128)(2,1)S(1)} %get-tuple-element.451), channel_id=1, source_target_pairs={{0,80},{8,88},{16,64},{24,72},{32,112},{40,120},{48,96},{56,104},{... | collective-permute-start | bytes 1179656 | tf_op jit(solution)/shard_map/ppermute | solution.py:204
  618.3 33.0 %collective-permute-start.10 = (bf16[1,2,64,1536]{3,2,1,0:T(8,128)(2,1)S(1)}, bf16[1,2,64,1536]{3,2,1,0:T(8,128)(2,1)S(1)}, u32[]{:S(2)}, u32[]{:S(2)}) collective-permute-start(bf16[1,2,64,1536]{3,2,1,0:T(8,128)(2,1)S(1)} %get-tuple-element.450), channel_id=1, source_target_pairs={{0,88},{8,80},{16,72},{24,64},{32,120},{40,112},{48,104},{56,96},{... | collective-permute-start | bytes 1179656 | tf_op jit(solution)/shard_map/ppermute | solution.py:204
  620.0 43.3 %collective-permute-start.11 = (bf16[1,2,64,1536]{3,2,1,0:T(8,128)(2,1)S(1)}, bf16[1,2,64,1536]{3,2,1,0:T(8,128)(2,1)S(1)}, u32[]{:S(2)}, u32[]{:S(2)}) collective-permute-start(bf16[1,2,64,1536]{3,2,1,0:T(8,128)(2,1)S(1)} %get-tuple-element.449), channel_id=1, source_target_pairs={{0,96},{8,104},{16,112},{24,120},{32,64},{40,72},{48,80},{56,88},{... | collective-permute-start | bytes 1179656 | tf_op jit(solution)/shard_map/ppermute | solution.py:204
  624.8 47.0 %collective-permute-start.12 = (bf16[1,2,64,1536]{3,2,1,0:T(8,128)(2,1)S(1)}, bf16[1,2,64,1536]{3,2,1,0:T(8,128)(2,1)S(1)}, u32[]{:S(2)}, u32[]{:S(2)}) collective-permute-start(bf16[1,2,64,1536]{3,2,1,0:T(8,128)(2,1)S(1)} %get-tuple-element.448), channel_id=1, source_target_pairs={{0,104},{8,96},{16,120},{24,112},{32,72},{40,64},{48,88},{56,80},{... | collective-permute-start | bytes 1179656 | tf_op jit(solution)/shard_map/ppermute | solution.py:204
  633.2 46.9 %collective-permute-start.13 = (bf16[1,2,64,1536]{3,2,1,0:T(8,128)(2,1)S(1)}, bf16[1,2,64,1536]{3,2,1,0:T(8,128)(2,1)S(1)}, u32[]{:S(2)}, u32[]{:S(2)}) collective-permute-start(bf16[1,2,64,1536]{3,2,1,0:T(8,128)(2,1)S(1)} %get-tuple-element.447), channel_id=1, source_target_pairs={{0,112},{8,120},{16,96},{24,104},{32,80},{40,88},{48,64},{56,72},{... | collective-permute-start | bytes 1179656 | tf_op jit(solution)/shard_map/ppermute | solution.py:204
  641.7 48.0 %collective-permute-start.14 = (bf16[1,2,64,1536]{3,2,1,0:T(8,128)(2,1)S(1)}, bf16[1,2,64,1536]{3,2,1,0:T(8,128)(2,1)S(1)}, u32[]{:S(2)}, u32[]{:S(2)}) collective-permute-start(bf16[1,2,64,1536]{3,2,1,0:T(8,128)(2,1)S(1)} %get-tuple-element.446), channel_id=1, source_target_pairs={{0,120},{8,112},{16,104},{24,96},{32,88},{40,80},{48,72},{56,64},{... | collective-permute-start | bytes 1179656 | tf_op jit(solution)/shard_map/ppermute | solution.py:204
  (20 other events, 61.0 us)
Sparse Core Ops, SparseCore 0:
  9.0 28.3 all-gather.1
  351.7 69.0 all-reduce.2
